TPU v7x, 256 devices: a whole 4x4x8 slice. The times are simulated.
256 devices in a mesh: row: 8 (over x_lo, y), col: 32 (over z, x_hi, core).
Axes of the slice: x: 4 (x_hi: 2, x_lo: 2; x = x_hi * 2 + x_lo), y: 4, z: 8, core: 2. Of those that a mesh axis runs over, the one named last changes fastest.
Arguments:
- frames: bfloat16 [1024, 8192], P('col', 'row'), may hold values from -6 to 6
- cotangent: bfloat16 [1024, 8192], P('col', 'row'), may hold values from -6 to 6
- gate_weight: bfloat16 [8192, 14336], P('row', 'col'), may hold values from -0.0625 to 0.0625
- up_weight: bfloat16 [8192, 14336], P('row', 'col'), may hold values from -0.0625 to 0.0625
- down_weight: bfloat16 [14336, 8192], P('col', 'row'), may hold values from -0.046875 to 0.046875
- utt_ids: int32 [1024], replicated, may hold values from 0 to 15, never falling along the last dimension, each value on 1 to 128 neighbouring positions
- valid_len: int32 [16], replicated, may hold values from 1 to 128
- time_start: int32 [16], replicated, may hold values from 0 to 127
- time_width: int32 [16], replicated, may hold values from 0 to 32
- freq_start: int32 [16], replicated, may hold values from 0 to 8191
- freq_width: int32 [16], replicated, may hold values from 0 to 2048
Outputs:
- output: bfloat16 [1024, 8192], P('col', 'row')
- grad_frames: bfloat16 [1024, 8192], P('col', 'row')
- grad_gate: bfloat16 [8192, 14336], P('row', 'col')
- grad_up: bfloat16 [8192, 14336], P('row', 'col')
- grad_down: bfloat16 [14336, 8192], P('col', 'row')
Inputs may be any that keep to these rules, and one draw needn't show every extreme that they name: `utt_ids`: token ids never fall along the tokens; each utterance holds 1 to 128 tokens.
All inputs are finite; a program needn't handle non-finite values.
Results may differ from a plain program's by a relative error of at most 0.025.
Values may be sent and summed in bfloat16 or wider, within the bound.
No kernel may reach another device: no remote copies, remote signals or barrier semaphores. Data moves between devices by JAX's collectives and lax.ppermute only.
A program may use at most 64 MiB of HBM per device.

v0:
```python
import jax
import jax.numpy as jnp
from jax import lax
from jax.sharding import PartitionSpec as P


def span_masks(
    utt_ids,
    local_ids,
    tok_index,
    feat_index,
    valid_len,
    time_start,
    time_width,
    freq_start,
    freq_width,
):
    utt_index = jnp.arange(valid_len.shape[0], dtype=jnp.int32)
    starts = jnp.sum((utt_ids[None, :] < utt_index[:, None]).astype(jnp.int32), axis=1)
    member = (local_ids[:, None] == utt_index[None, :]).astype(jnp.int32)

    def lookup(table):
        return jnp.sum(member * table[None, :], axis=1)

    position = tok_index - lookup(starts)
    valid_rows = position < lookup(valid_len)
    time_low = lookup(time_start)
    in_time = (position >= time_low) & (position < time_low + lookup(time_width))
    freq_low = lookup(freq_start)[:, None]
    freq_high = freq_low + lookup(freq_width)[:, None]
    in_freq = (feat_index[None, :] >= freq_low) & (feat_index[None, :] < freq_high)
    keep_mask = (valid_rows & jnp.logical_not(in_time))[:, None] & jnp.logical_not(in_freq)
    return (keep_mask, valid_rows)


def shards(
    frames,
    cotangent,
    gate_weight,
    up_weight,
    down_weight,
    utt_ids,
    valid_len,
    time_start,
    time_width,
    freq_start,
    freq_width,
):
    tok_rows, feat_cols = frames.shape
    hidden_cols = gate_weight.shape[1]
    first_tok = lax.axis_index("col") * tok_rows
    first_feat = lax.axis_index("row") * feat_cols
    tok_index = first_tok + jnp.arange(tok_rows, dtype=jnp.int32)
    feat_index = first_feat + jnp.arange(feat_cols, dtype=jnp.int32)
    local_ids = lax.dynamic_slice_in_dim(utt_ids, first_tok, tok_rows)
    keep_mask, valid_rows = span_masks(
        utt_ids,
        local_ids,
        tok_index,
        feat_index,
        valid_len,
        time_start,
        time_width,
        freq_start,
        freq_width,
    )
    masked = jnp.where(keep_mask, frames, jnp.zeros_like(frames))
    cot_valid = jnp.where(valid_rows[:, None], cotangent, jnp.zeros_like(cotangent))
    contract_last = (((1,), (1,)), ((), ()))
    contract_first = (((0,), (0,)), ((), ()))
    both_all = lax.all_gather(
        jnp.concatenate([masked, cot_valid], axis=1), "col", axis=0, tiled=True
    )
    tokens_all = both_all[:, :feat_cols]
    cot_all = both_all[:, feat_cols:]
    sums = lax.psum_scatter(
        jnp.concatenate(
            [
                jnp.dot(tokens_all, gate_weight, preferred_element_type=jnp.float32),
                jnp.dot(tokens_all, up_weight, preferred_element_type=jnp.float32),
                lax.dot_general(
                    cot_all, down_weight, contract_last, preferred_element_type=jnp.float32
                ),
            ],
            axis=1,
        ).astype(jnp.bfloat16),
        "row",
        scatter_dimension=0,
        tiled=True,
    ).astype(jnp.float32)
    gate = sums[:, :hidden_cols]
    up = sums[:, hidden_cols : 2 * hidden_cols]
    grad_hidden = sums[:, 2 * hidden_cols :]
    sigmoid_gate = jax.nn.sigmoid(gate)
    hidden = (gate * sigmoid_gate * up).astype(jnp.bfloat16)
    dgate = (grad_hidden * up * sigmoid_gate * (1.0 + gate * (1.0 - sigmoid_gate))).astype(
        jnp.bfloat16
    )
    dup = (grad_hidden * gate * sigmoid_gate).astype(jnp.bfloat16)
    acts_all = lax.all_gather(
        jnp.concatenate([hidden, dgate, dup], axis=1), "row", axis=0, tiled=True
    )
    hidden_all = acts_all[:, :hidden_cols]
    dgate_all = acts_all[:, hidden_cols : 2 * hidden_cols]
    dup_all = acts_all[:, 2 * hidden_cols :]
    grad_down = lax.dot_general(
        hidden_all, cot_all, contract_first, preferred_element_type=jnp.float32
    ).astype(jnp.bfloat16)
    grad_gate = lax.dot_general(
        tokens_all, dgate_all, contract_first, preferred_element_type=jnp.float32
    ).astype(jnp.bfloat16)
    grad_up = lax.dot_general(
        tokens_all, dup_all, contract_first, preferred_element_type=jnp.float32
    ).astype(jnp.bfloat16)
    out_sums = lax.psum_scatter(
        jnp.concatenate(
            [
                jnp.dot(hidden_all, down_weight, preferred_element_type=jnp.float32).astype(
                    jnp.bfloat16
                ),
                (
                    lax.dot_general(
                        dgate_all, gate_weight, contract_last, preferred_element_type=jnp.float32
                    )
                    + lax.dot_general(
                        dup_all, up_weight, contract_last, preferred_element_type=jnp.float32
                    )
                ).astype(jnp.bfloat16),
            ],
            axis=1,
        ),
        "col",
        scatter_dimension=0,
        tiled=True,
    )
    output = out_sums[:, :feat_cols]
    grad_masked = out_sums[:, feat_cols:].astype(jnp.float32)
    grad_frames = jnp.where(keep_mask, grad_masked, jnp.zeros_like(grad_masked)).astype(
        jnp.bfloat16
    )
    return (output, grad_frames, grad_gate, grad_up, grad_down)


def solution(mesh):
    placed = (
        P("col", "row"),
        P("col", "row"),
        P("row", "col"),
        P("row", "col"),
        P("col", "row"),
        P(),
        P(),
        P(),
        P(),
        P(),
        P(),
    )
    return jax.shard_map(
        shards,
        mesh=mesh,
        in_specs=placed,
        out_specs=(
            P("col", "row"),
            P("col", "row"),
            P("row", "col"),
            P("row", "col"),
            P("col", "row"),
        ),
        check_vma=False,
    )
```

profile of v0, /device:TPU:8, one launch (start us, length us, event | category | flops | bytes accessed | tf_op | source)
XLA Modules:
  0.0 367.0 jit_solution(1127609087687936519)
XLA Ops:
  7.2 0.9 convert_reduce_fusion
  8.2 0.8 dynamic_slice.3
  8.9 1.0 copy.26
  10.0 1.0 copy.27
  11.0 0.8 select_reduce_fusion.2
  13.1 89.6 %all-gather.3.cloned.1.call-done = bf16[1024,2048]{1,0:T(8,128)(2,1)} async-done(((bf16[32,2048]{1,0:T(8,128)(2,1)}), bf16[1024,2048]{1,0:T(8,128)(2,1)}) %all-gather.3.cloned.1.call-update) | async-done | bytes 4194320 | tf_op jit(solution)/shard_map/all_gather | solution.py:71
  102.7 2.9 convolution_convert_fusion.3
  105.6 1.2 fusion.4
  106.8 1.2 convolution_convert_fusion.4
  107.9 1.8 pad_maximum_fusion.1
  109.8 4.5 %copy.32 = bf16[1024,1344]{1,0:T(8,128)(2,1)} copy(bf16[1024,1344]{0,1:T(8,128)(2,1)} %pad_maximum_fusion.1) | data formatting | bytes 5505024
  114.4 43.0 %reduce-scatter.7.cloned.1.call-done = bf16[128,1344]{1,0:T(8,128)(2,1)} async-done(((bf16[1024,1344]{1,0:T(8,128)(2,1)}), bf16[128,1344]{1,0:T(8,128)(2,1)}) %reduce-scatter.7.cloned.1.call-update) | async-done | bytes 344080
  157.4 1.2 copy.33
  159.9 54.0 %all-gather.5.cloned.1.call-done = bf16[1024,1344]{0,1:T(8,128)(2,1)} async-done(((bf16[128,1344]{0,1:T(8,128)(2,1)}), bf16[1024,1344]{0,1:T(8,128)(2,1)}) %all-gather.5.cloned.1.call-update) | async-done | bytes 2752528 | tf_op jit(solution)/shard_map/all_gather | solution.py:100
  213.8 2.6 convolution_convert_fusion
  216.5 1.4 fusion.17
  217.8 1.4 add_convert_fusion
  219.3 2.4 pad_maximum_fusion
  221.7 6.5 %copy.34 = bf16[1024,2048]{1,0:T(8,128)(2,1)} copy(bf16[1024,2048]{0,1:T(8,128)(2,1)} %pad_maximum_fusion) | data formatting | bytes 8388608
  228.3 4.1 %fusion.7 = bf16[448,1024]{1,0:T(8,128)(2,1)} fusion(bf16[1024,2048]{1,0:T(8,128)(2,1)} %all-gather.3.cloned.1.call-done, bf16[1024,1344]{0,1:T(8,128)(2,1)} %all-gather.5.cloned.1.call-done), kind=kOutput, calls=%fused_computation.9 | convolution fusion | flops 939982848 | bytes 3932160 | tf_op jit(solution)/shard_map/dot_general | solution.py:106
  232.3 2.1 convolution_convert_fusion.2
  234.4 2.0 convolution_convert_fusion.1
  236.4 121.4 %reduce-scatter.9.cloned.1.call-done = bf16[32,2048]{1,0:T(8,128)(2,1)} async-done(((bf16[1024,2048]{1,0:T(8,128)(2,1)}), bf16[32,2048]{1,0:T(8,128)(2,1)}) %reduce-scatter.9.cloned.1.call-update) | async-done | bytes 131088
  357.8 1.5 fusion.23
  (37 shorter events, 3.8 us)
Async XLA Ops:
  7.2 98.4 %copy-start = (bf16[448,1024]{1,0:T(8,128)(2,1)S(1)}, bf16[448,1024]{1,0:T(8,128)(2,1)}, u32[]{:S(2)}) copy-start(bf16[448,1024]{1,0:T(8,128)(2,1)} %param.15) | copy-start | bytes 2752516
  7.2 95.5 %copy-start.1 = (bf16[1024,448]{0,1:T(8,128)(2,1)S(1)}, bf16[1024,448]{0,1:T(8,128)(2,1)}, u32[]{:S(2)}) copy-start(bf16[1024,448]{0,1:T(8,128)(2,1)} %param.14) | copy-start | bytes 2752516
  7.2 95.5 %all-gather.3.cloned.1.call-start = ((), (), s32[]{:S(2)}) async-start(), calls=%async_computation.2 | async-start | bytes 4325376 | tf_op jit(solution)/shard_map/all_gather | solution.py:71
  13.1 144.4 %reduce-scatter.7.cloned.1.call-start = ((), (), s32[]{:S(2)}) async-start(), calls=%async_computation.4 | async-start | bytes 3244032
  102.7 2.9 copy-start.4
  105.6 1.2 copy-start.6
  114.3 99.5 %all-gather.5.cloned.1.call-start = ((), (), s32[]{:S(2)}) async-start(), calls=%async_computation.3 | async-start | bytes 3096576 | tf_op jit(solution)/shard_map/all_gather | solution.py:100
  159.6 56.8 %copy-start.7 = (bf16[1024,448]{0,1:T(8,128)(2,1)S(1)}, bf16[1024,448]{0,1:T(8,128)(2,1)}, u32[]{:S(2)}) copy-start(bf16[1024,448]{0,1:T(8,128)(2,1)} %param.13) | copy-start | bytes 2752516
  159.6 198.2 %reduce-scatter.9.cloned.1.call-start = ((), (), s32[]{:S(2)}) async-start(), calls=%async_computation.5 | async-start | bytes 4325376
  213.8 2.6 copy-start.2
  228.2 4.1 %copy-start.3 = (bf16[1024,1344]{0,1:T(8,128)(2,1)S(1)}, bf16[1024,1344]{0,1:T(8,128)(2,1)}, u32[]{:S(2)}) copy-start(bf16[1024,1344]{0,1:T(8,128)(2,1)} %all-gather.5.cloned.1.call-done) | copy-start | bytes 8257540
  228.2 4.1 %copy-start.5 = (bf16[1024,2048]{1,0:T(8,128)(2,1)S(1)}, bf16[1024,2048]{1,0:T(8,128)(2,1)}, u32[]{:S(2)}) copy-start(bf16[1024,2048]{1,0:T(8,128)(2,1)} %all-gather.3.cloned.1.call-done) | copy-start | bytes 12582916
Sparse Core Ops, SparseCore 0:
  13.2 89.4 all-gather.2
  114.5 42.9 reduce-scatter.6
  159.7 54.0 all-gather.4
  228.4 129.3 reduce-scatter.8
where the time goes:
time: 368 us; the launch traced here: 367 us
  waiting for transfers between devices  308 us (84%)
  matrix products  18.8 us (5%)
  local copies, waits for them, and re-layouts  17.7 us (5%)
  between operations  14 us (4%)
  other arithmetic  8.17 us (2%)
    unnamed x6, waiting for transfers between devices  164 us
    all_gather x1, waiting for transfers between devices, shards(): lax.all_gather(jnp.concatenate([masked, cot_valid], axis=1), 'col', axis=...  89.6 us
    all_gather x1, waiting for transfers between devices, shards(): lax.all_gather(jnp.concatenate([hidden, dgate, dup], axis=1), 'row', axis...  54 us
    unnamed x23, local copies, waits for them, and re-layouts  15.2 us
  transfers between devices with their start and end apart: 4, of which 4 were waited for; matrix products, arithmetic and copies ran while one was open for 2% of the time, Pallas kernels for 0%

commit v1 on v0

--- a/solution.py
+++ b/solution.py
@@ -97,9 +97,9 @@
         jnp.bfloat16
     )
     dup = (grad_hidden * gate * sigmoid_gate).astype(jnp.bfloat16)
-    acts_all = lax.all_gather(
-        jnp.concatenate([hidden, dgate, dup], axis=1), "row", axis=0, tiled=True
-    )
+    block = jnp.concatenate([hidden, dgate, dup], axis=1)
+    sent = jnp.stack([block] * lax.axis_size("row"))
+    acts_all = jnp.concatenate(lax.all_to_all(sent, "row", 0, 0), axis=0)
     hidden_all = acts_all[:, :hidden_cols]
     dgate_all = acts_all[:, hidden_cols : 2 * hidden_cols]
     dup_all = acts_all[:, 2 * hidden_cols :]

time: 368 us -> 346 us (0.940)
  waiting for transfers between devices: 308 us -> 253 us
  blocking collectives: 0 us -> 33.9 us
    all_gather x1 -> x0, waiting for transfers between devices: 54 us -> none  [shards(): lax.all_gather(jnp.concatenate([hidden, dgate, dup], axis=1), 'row', axis...]
    all_to_all x0 -> x1, blocking collectives: none -> 33.9 us  [shards(): acts_all = jnp.concatenate(lax.all_to_all(sent, 'row', 0, 0), axis=0)]
    unnamed x6 -> x5, waiting for transfers between devices: 164 us -> 164 us
  transfers between devices with their start and end apart: 4 -> 3, of which waited for: 4 -> 3; matrix products, arithmetic and copies ran while one was open for 2% -> 2% of each run, Pallas kernels for 0% -> 0%
where the time goes in v1:
time: 346 us; the launch traced here: 345 us
  waiting for transfers between devices  253 us (73%)
  blocking collectives  33.9 us (10%)
  local copies, waits for them, and re-layouts  19 us (5%)
  matrix products  17.3 us (5%)
  between operations  14 us (4%)
  other arithmetic  7.45 us (2%)
    unnamed x5, waiting for transfers between devices  164 us
    all_gather x1, waiting for transfers between devices, shards(): lax.all_gather(jnp.concatenate([masked, cot_valid], axis=1), 'col', axis=...  89.6 us
    all_to_all x1, blocking collectives, shards(): acts_all = jnp.concatenate(lax.all_to_all(sent, 'row', 0, 0), axis=0)  33.9 us
    unnamed x23, local copies, waits for them, and re-layouts  15.7 us
  transfers between devices with their start and end apart: 3, of which 3 were waited for; matrix products, arithmetic and copies ran while one was open for 2% of the time, Pallas kernels for 0%

profile of v1, /device:TPU:8, one launch (start us, length us, event | category | flops | bytes accessed | tf_op | source)
XLA Modules:
  0.0 345.0 jit_solution(7296411597547787419)
XLA Ops:
  7.2 0.9 convert_reduce_fusion
  8.2 0.8 dynamic_slice.3
  8.9 1.0 copy.34
  10.0 1.0 copy.35
  11.0 0.8 select_reduce_fusion.2
  13.1 89.6 %all-gather.2.cloned.1.call-done = bf16[1024,2048]{1,0:T(8,128)(2,1)} async-done(((bf16[32,2048]{1,0:T(8,128)(2,1)}), bf16[1024,2048]{1,0:T(8,128)(2,1)}) %all-gather.2.cloned.1.call-update) | async-done | bytes 4194320 | tf_op jit(solution)/shard_map/all_gather | solution.py:71
  102.7 2.9 convolution_convert_fusion.3
  105.6 1.2 fusion.4
  106.8 1.2 convolution_convert_fusion.4
  107.9 1.8 pad_maximum_fusion.1
  109.8 4.5 %copy.41 = bf16[1024,1344]{1,0:T(8,128)(2,1)} copy(bf16[1024,1344]{0,1:T(8,128)(2,1)} %pad_maximum_fusion.1) | data formatting | bytes 5505024
  114.4 43.1 %reduce-scatter.7.cloned.1.call-done = bf16[128,1344]{1,0:T(8,128)(2,1)} async-done(((bf16[1024,1344]{1,0:T(8,128)(2,1)}), bf16[128,1344]{1,0:T(8,128)(2,1)}) %reduce-scatter.7.cloned.1.call-update) | async-done | bytes 344080
  157.5 1.2 copy.42
  159.3 33.9 %all_to_all.5 = bf16[8,128,1344]{1,2,0:T(8,128)(2,1)S(1)} all-to-all(bf16[8,128,1344]{1,2,0:T(8,128)(2,1)S(1)} %stack.2), channel_id=1, replica_groups=mesh['row'=8,'col'=32] {'row'}, dimensions={0} | all-to-all | bytes 5505024 | tf_op jit(solution)/shard_map/all_to_all | solution.py:102
  193.6 1.3 convolution_convert_fusion
  195.4 1.3 fusion.17
  196.7 1.3 add_convert_fusion
  198.0 2.4 pad_maximum_fusion
  200.5 6.5 %copy.43 = bf16[1024,2048]{1,0:T(8,128)(2,1)} copy(bf16[1024,2048]{0,1:T(8,128)(2,1)} %pad_maximum_fusion) | data formatting | bytes 8388608
  207.0 4.1 %fusion.7 = bf16[448,1024]{1,0:T(8,128)(2,1)} fusion(bf16[1024,2048]{1,0:T(8,128)(2,1)} %all-gather.2.cloned.1.call-done, bf16[1024,1344]{0,1:T(8,128)(2,1)} %copy-done.1), kind=kOutput, calls=%fused_computation.10 | convolution fusion | flops 939982848 | bytes 3932160 | tf_op jit(solution)/shard_map/dot_general | solution.py:106
  211.1 2.1 convolution_convert_fusion.2
  213.1 2.0 convolution_convert_fusion.1
  215.2 120.6 %reduce-scatter.9.cloned.1.call-done = bf16[32,2048]{1,0:T(8,128)(2,1)} async-done(((bf16[1024,2048]{1,0:T(8,128)(2,1)}), bf16[32,2048]{1,0:T(8,128)(2,1)}) %reduce-scatter.9.cloned.1.call-update) | async-done | bytes 131088
  335.8 1.5 fusion.23
  (37 shorter events, 4.1 us)
Async XLA Ops:
  7.2 98.4 %copy-start = (bf16[448,1024]{1,0:T(8,128)(2,1)S(1)}, bf16[448,1024]{1,0:T(8,128)(2,1)}, u32[]{:S(2)}) copy-start(bf16[448,1024]{1,0:T(8,128)(2,1)} %param.15) | copy-start | bytes 2752516
  7.2 95.5 %copy-start.3 = (bf16[1024,448]{0,1:T(8,128)(2,1)S(1)}, bf16[1024,448]{0,1:T(8,128)(2,1)}, u32[]{:S(2)}) copy-start(bf16[1024,448]{0,1:T(8,128)(2,1)} %param.14) | copy-start | bytes 2752516
  7.2 95.5 %all-gather.2.cloned.1.call-start = ((), (), s32[]{:S(2)}) async-start(), calls=%async_computation.3 | async-start | bytes 4325376 | tf_op jit(solution)/shard_map/all_gather | solution.py:71
  13.1 144.4 %reduce-scatter.7.cloned.1.call-start = ((), (), s32[]{:S(2)}) async-start(), calls=%async_computation.4 | async-start | bytes 3244032
  102.7 2.9 copy-start.4
  105.6 1.2 copy-start.6
  114.3 221.5 %reduce-scatter.9.cloned.1.call-start = ((), (), s32[]{:S(2)}) async-start(), calls=%async_computation.5 | async-start | bytes 4325376
  193.6 3.2 copy-start.1
  193.6 1.8 copy-start.7
  207.0 4.1 %copy-start.2 = (bf16[1024,1344]{0,1:T(8,128)(2,1)S(1)}, bf16[1024,1344]{0,1:T(8,128)(2,1)}, u32[]{:S(2)}) copy-start(bf16[1024,1344]{0,1:T(8,128)(2,1)} %copy-done.1) | copy-start | bytes 8257540
  207.0 4.1 %copy-start.5 = (bf16[1024,2048]{1,0:T(8,128)(2,1)S(1)}, bf16[1024,2048]{1,0:T(8,128)(2,1)}, u32[]{:S(2)}) copy-start(bf16[1024,2048]{1,0:T(8,128)(2,1)} %all-gather.2.cloned.1.call-done) | copy-start | bytes 12582916
Sparse Core Ops, SparseCore 0:
  13.2 89.4 all-gather.1
  114.5 42.9 reduce-scatter.6
  207.1 128.6 reduce-scatter.8
